TPU v7x, 256 devices: a whole 4x4x8 slice. The times are simulated.
256 devices in a mesh: leaf: 2 (over core), row: 8 (over z), col: 16 (over y, x).
Axes of the slice: x: 4, y: 4, z: 8, core: 2. Of those that a mesh axis runs over, the one named last changes fastest.
Arguments:
- front: float32 [2, 8, 8, 128, 4, 16, 128], P('leaf', None, 'row', None, None, 'col'), as said below
- parent: float32 [4, 2, 8, 128, 4, 16, 128], P(None, 'leaf', 'row', None, None, 'col'), may hold values from -0.2 to 0.2
- tile_map: int32 [2, 56], replicated, may hold values from 0 to 63, as said below
- col_shift: int32 [4], replicated, may hold values from 0 to 7
Outputs:
- factored: float32 [2, 8, 8, 128, 4, 16, 128], P('leaf', None, 'row', None, None, 'col')
- new_parent: float32 [4, 2, 8, 128, 4, 16, 128], P(None, 'leaf', 'row', None, None, 'col')
Inputs may be any that keep to these rules, and one draw needn't show every extreme that they name: For each leaf the 8192 x 8192 matrix read from front is symmetric positive definite. Entry [l, e] names the parent tile joined by tile 8 + e of child l; no row repeats a value. The parent tile q = tile_map[l, e] has (q mod 16 + col_shift[q // 16]) mod 16 equal to (8 + e) mod 16. Among the tiles of one child whose indices are equal mod 8, at most 1 have parent tiles equal mod 16.
All inputs are finite; a program needn't handle non-finite values.
Results may differ from a plain program's by a relative error of at most 0.0001.
Values sent between devices are 32-bit elements; how exact they have to be, the bound alone decides.
No kernel may reach another device: no remote copies, remote signals or barrier semaphores. Data moves between devices by JAX's collectives and lax.ppermute only.
A program may use at most 128 MiB of HBM per device.

v0:
```python
import jax
import jax.numpy as jnp
from jax import lax
from jax.sharding import PartitionSpec as P

TILE = 128
PB = 512
PANELS = 2
NPIV = 1024
HIGHEST = lax.Precision.HIGHEST


def spread(value, axis, source):
    kept = jnp.where(lax.axis_index(axis) == source, value, 0).astype(value.dtype)
    return lax.psum(kept, axis)


def update_slots(working, next_rows, column_factor, slot_low, slot_high):
    product = jnp.einsum(
        "atp,bsp->atbs",
        next_rows,
        column_factor,
        precision=HIGHEST,
        preferred_element_type=jnp.float32,
    )
    return working.at[:, :, slot_low:slot_high, :].add(-product)


def per_device(front, parent, tile_map, col_shift):
    leaf_count = lax.axis_size("leaf")
    row_count = lax.axis_size("row")
    col_count = lax.axis_size("col")
    leaf_index = lax.axis_index("leaf")
    row_index = lax.axis_index("row")
    col_index = lax.axis_index("col")
    local_front = front[0, :, 0, :, :, 0, :]
    row_slots = local_front.shape[0]
    col_slots = local_front.shape[2]
    pivot_tiles = NPIV // TILE
    assert pivot_tiles == row_count and pivot_tiles <= col_count
    row_tiles = jnp.arange(row_slots, dtype=jnp.int32) * row_count + row_index
    col_tiles = jnp.arange(col_slots, dtype=jnp.int32) * col_count + col_index
    working = local_front
    top_rows = lax.all_gather(working[0], "row", axis=0, tiled=False)
    column_panel = top_rows.transpose(2, 3, 0, 1).reshape(col_slots, TILE, NPIV)
    first_cols = lax.all_gather(working[:, :, 0, :], "col", axis=0, tiled=False)
    row_panel = first_cols[:pivot_tiles].transpose(1, 2, 0, 3).reshape(row_slots, TILE, NPIV)
    diagonal_block = lax.all_gather(row_panel[0], "row", axis=0, tiled=True)
    lower_factor = jnp.linalg.cholesky(diagonal_block)
    stacked = jnp.concatenate(
        [row_panel[1:].reshape(-1, NPIV), column_panel.reshape(-1, NPIV)], axis=0
    )
    solved = lax.linalg.triangular_solve(
        lower_factor, stacked, left_side=False, lower=True, transpose_a=True
    )
    trailing_rows = (row_slots - 1) * TILE
    row_factor = solved[:trailing_rows].reshape(row_slots - 1, TILE, NPIV)
    column_factor = solved[trailing_rows:].reshape(col_slots, TILE, NPIV)
    column_factor = jnp.where((col_tiles >= pivot_tiles)[:, None, None], column_factor, 0.0)
    product = jnp.einsum(
        "atk,bsk->atbs",
        row_factor,
        column_factor,
        precision=HIGHEST,
        preferred_element_type=jnp.float32,
    )
    trailing = working[1:] - product
    own_col = jnp.minimum(col_index, pivot_tiles - 1)
    row_factor_cols = lax.dynamic_slice_in_dim(row_factor, own_col * TILE, TILE, 2)
    is_factor_col = (col_tiles < pivot_tiles)[None, None, :, None]
    trailing = jnp.where(is_factor_col, row_factor_cols[:, :, None, :], trailing)
    diag_rows = lax.dynamic_slice_in_dim(lower_factor, row_index * TILE, TILE, 0)
    diag_tile = lax.dynamic_slice_in_dim(diag_rows, own_col * TILE, TILE, 1)
    local_ids = jnp.arange(TILE, dtype=jnp.int32)
    global_row = row_index * TILE + local_ids[:, None]
    global_col = own_col * TILE + local_ids[None, :]
    diag_tile = jnp.where(global_row >= global_col, diag_tile, 0.0)
    top = jnp.where(is_factor_col[0], diag_tile[:, None, :], 0.0)
    top = jnp.broadcast_to(top, working[0].shape)
    working = jnp.concatenate([top[None], trailing], axis=0)
    factored = working.reshape(front.shape)
    contribution = jnp.where((col_tiles >= pivot_tiles)[None, None, :, None], working, 0.0)
    contrib_count = tile_map.shape[1]
    entry_ids = jnp.arange(contrib_count, dtype=jnp.int32)
    own_map = lax.dynamic_index_in_dim(tile_map, leaf_index, 0, keepdims=False)
    row_match = (row_tiles - pivot_tiles)[:, None] == entry_ids[None, :]
    row_targets = jnp.sum(jnp.where(row_match, own_map[None, :], 0), axis=1)
    row_valid = row_tiles >= pivot_tiles
    owner_count = leaf_count * row_count
    destination = row_targets % owner_count
    parent_row_slot = row_targets // owner_count
    slot_ids = jnp.arange(row_slots, dtype=jnp.int32)
    same_before = (
        (destination[None, :] == destination[:, None])
        & row_valid[None, :]
        & (slot_ids[None, :] < slot_ids[:, None])
    )
    rank_in_dest = jnp.sum(same_before.astype(jnp.int32), axis=1)
    capacity = (col_slots + row_count - 1) // row_count
    owner_ids = jnp.arange(owner_count, dtype=jnp.int32)
    capacity_ids = jnp.arange(capacity, dtype=jnp.int32)
    selection = (
        row_valid[None, None, :]
        & (destination[None, None, :] == owner_ids[:, None, None])
        & (rank_in_dest[None, None, :] == capacity_ids[None, :, None])
    )
    flattened = contribution.reshape(row_slots, -1)
    send_buffer = jnp.einsum(
        "oka,ax->okx",
        selection.astype(jnp.float32),
        flattened,
        precision=HIGHEST,
        preferred_element_type=jnp.float32,
    )
    chosen_slot = jnp.sum(jnp.where(selection, parent_row_slot[None, None, :], 0), axis=2)
    send_slots = jnp.where(jnp.any(selection, axis=2), chosen_slot, -1)
    received, received_slots = (
        lax.all_to_all(send_buffer, ("leaf", "row"), split_axis=0, concat_axis=0, tiled=True),
        lax.all_to_all(send_slots, ("leaf", "row"), split_axis=0, concat_axis=0, tiled=True),
    )
    received = received.reshape(leaf_count, row_count, capacity, -1)
    received_slots = received_slots.reshape(leaf_count, row_count, capacity)
    parent_local = parent[:, 0, 0, :, :, 0, :]
    parent_rows = parent_local.shape[0]
    parent_cols = parent_local.shape[2]
    row_place = (
        received_slots[None] == jnp.arange(parent_rows, dtype=jnp.int32)[:, None, None, None]
    ).astype(jnp.float32)
    by_leaf = jnp.einsum(
        "slrk,lrkx->slx", row_place, received, precision=HIGHEST, preferred_element_type=jnp.float32
    )
    by_leaf = by_leaf.reshape(parent_rows, leaf_count, TILE, col_slots, TILE)
    col_match = (col_tiles - pivot_tiles)[:, None] == entry_ids[None, :]
    col_targets = jnp.sum(jnp.where(col_match[None], tile_map[:, None, :], 0), axis=2)
    col_valid = col_tiles >= pivot_tiles
    parent_slot_ids = jnp.arange(parent_cols, dtype=jnp.int32)
    col_place = (
        col_valid[None, None, :]
        & (col_targets[:, None, :] // col_count == parent_slot_ids[None, :, None])
    ).astype(jnp.float32)
    assembled = jnp.einsum(
        "sltbv,lub->stuv", by_leaf, col_place, precision=HIGHEST, preferred_element_type=jnp.float32
    )
    new_parent = (parent_local + assembled).reshape(parent.shape)
    return (factored, new_parent)


def solution(mesh):
    return jax.shard_map(
        per_device,
        mesh=mesh,
        in_specs=(
            P("leaf", None, "row", None, None, "col", None),
            P(None, "leaf", "row", None, None, "col", None),
            P(),
            P(),
        ),
        out_specs=(
            P("leaf", None, "row", None, None, "col", None),
            P(None, "leaf", "row", None, None, "col", None),
        ),
        check_vma=False,
    )
```

profile of v0, /device:TPU:1, one launch (start us, length us, event | category | flops | bytes accessed | tf_op | source)
XLA Modules:
  0.0 730.9 jit_solution(1884247141406783807)
XLA Ops:
  12.2 78.9 %all-gather.8.cloned.1.call-done = f32[128,128,1,128]{3,1,2,0:T(8,128)} async-done(((f32[8,128,1,128]{3,1,2,0:T(8,128)}), f32[128,128,1,128]{3,1,2,0:T(8,128)}) %all-gather.8.cloned.1.call-update) | async-done | bytes 8388624 | tf_op jit(solution)/shard_map/all_gather | solution.py:46
  91.0 2.2 slice-done
  93.2 2.4 copy.88
  99.9 7.7 %all-to-all-start.1 = ((s32[16,1,1]{2,1,0:T(1,128)}), s32[16,1,1]{2,1,0:T(1,128)S(1)}, u32[]{:S(2)}, u32[]{:S(2)}) async-start(s32[16,1,1]{2,1,0:T(1,128)} %copy.67), calls=%async_computation.1 | async-start | bytes 16384 | tf_op jit(solution)/shard_map/all_to_all | solution.py:119
  107.8 22.4 %all-gather.10.cloned.1.call-done = f32[8,1,1,128,4,1,128]{6,3,5,4,2,1,0:T(8,128)} async-done(((f32[1,1,1,128,4,1,128]{6,3,5,4,2,1,0:T(8,128)}), f32[8,1,1,128,4,1,128]{6,3,5,4,2,1,0:T(8,128)}) %all-gather.10.cloned.1.call-update) | async-done | bytes 2097168 | tf_op jit(solution)/shard_map/all_gather | solution.py:44
  132.2 2.3 slice.280
  134.5 2.7 bitcast_dynamic-update-slice_fusion.1
  139.0 55.7 %all-gather.6.cloned.1.call-done = f32[1024,1024]{0,1:T(8,128)} async-done(((f32[128,1024]{0,1:T(8,128)}), f32[1024,1024]{0,1:T(8,128)}) %all-gather.6.cloned.1.call-update) | async-done | bytes 4194320 | tf_op jit(solution)/shard_map/all_gather | solution.py:48
  194.6 5.5 copy.59
  200.2 4.4 fusion.2
  206.6 11.7 %cholesky.223 = f32[128,128]{1,0:T(8,128)S(1)} custom-call(f32[128,128]{1,0:T(8,128)S(1)} %cholesky.580), custom_call_target="Cholesky" | custom-call | tf_op jit(solution)/shard_map/jit(cholesky)/cholesky | solution.py:49
  218.4 9.8 %custom-call.62 = f32[1,128,128]{1,2,0:T(8,128)S(1)} custom-call(f32[1,128,128]{2,1,0:T(8,128)S(1)} %get-tuple-element.80), custom_call_target="InvertDiagBlocksLowerTriangular" | custom-call | tf_op jit(solution)/shard_map/jit(cholesky)/cholesky | solution.py:49
  228.2 2.5 cholesky.255
  230.7 2.4 constant_dynamic-update-slice_fusion.30
  234.6 11.9 %cholesky.244 = f32[128,128]{1,0:T(8,128)S(1)} custom-call(f32[128,128]{1,0:T(8,128)S(1)} %cholesky.584), custom_call_target="Cholesky" | custom-call | tf_op jit(solution)/shard_map/jit(cholesky)/cholesky | solution.py:49
  247.2 9.8 %custom-call.63 = f32[1,128,128]{1,2,0:T(8,128)S(1)} custom-call(f32[1,128,128]{2,1,0:T(8,128)S(1)} %get-tuple-element.77), custom_call_target="InvertDiagBlocksLowerTriangular" | custom-call | tf_op jit(solution)/shard_map/jit(cholesky)/cholesky | solution.py:49
  258.2 2.1 convolution_subtract_fusion.7
  260.3 11.7 %cholesky.468 = f32[128,128]{1,0:T(8,128)S(1)} custom-call(f32[128,128]{1,0:T(8,128)S(1)} %cholesky.589), custom_call_target="Cholesky" | custom-call | tf_op jit(solution)/shard_map/jit(cholesky)/cholesky | solution.py:49
  273.3 9.8 %custom-call.64 = f32[1,128,128]{1,2,0:T(8,128)S(1)} custom-call(f32[1,128,128]{2,1,0:T(8,128)S(1)} %get-tuple-element.74), custom_call_target="InvertDiagBlocksLowerTriangular" | custom-call | tf_op jit(solution)/shard_map/jit(cholesky)/cholesky | solution.py:49
  284.3 2.3 convolution_subtract_fusion.8
  286.7 12.1 %cholesky.487 = f32[128,128]{1,0:T(8,128)S(1)} custom-call(f32[128,128]{1,0:T(8,128)S(1)} %cholesky.594), custom_call_target="Cholesky" | custom-call | tf_op jit(solution)/shard_map/jit(cholesky)/cholesky | solution.py:49
  300.0 9.8 %custom-call.65 = f32[1,128,128]{1,2,0:T(8,128)S(1)} custom-call(f32[1,128,128]{2,1,0:T(8,128)S(1)} %get-tuple-element.71), custom_call_target="InvertDiagBlocksLowerTriangular" | custom-call | tf_op jit(solution)/shard_map/jit(cholesky)/cholesky | solution.py:49
  310.9 2.3 convolution_subtract_fusion.9
  313.3 11.7 %cholesky.506 = f32[128,128]{1,0:T(8,128)S(1)} custom-call(f32[128,128]{1,0:T(8,128)S(1)} %cholesky.599), custom_call_target="Cholesky" | custom-call | tf_op jit(solution)/shard_map/jit(cholesky)/cholesky | solution.py:49
  326.4 9.9 %custom-call.66 = f32[1,128,128]{1,2,0:T(8,128)S(1)} custom-call(f32[1,128,128]{2,1,0:T(8,128)S(1)} %get-tuple-element.68), custom_call_target="InvertDiagBlocksLowerTriangular" | custom-call | tf_op jit(solution)/shard_map/jit(cholesky)/cholesky | solution.py:49
  337.3 2.3 convolution_subtract_fusion.10
  339.6 11.7 %cholesky.526 = f32[128,128]{1,0:T(8,128)S(1)} custom-call(f32[128,128]{1,0:T(8,128)S(1)} %cholesky.604), custom_call_target="Cholesky" | custom-call | tf_op jit(solution)/shard_map/jit(cholesky)/cholesky | solution.py:49
  352.6 9.8 %custom-call.67 = f32[1,128,128]{1,2,0:T(8,128)S(1)} custom-call(f32[1,128,128]{2,1,0:T(8,128)S(1)} %get-tuple-element.65), custom_call_target="InvertDiagBlocksLowerTriangular" | custom-call | tf_op jit(solution)/shard_map/jit(cholesky)/cholesky | solution.py:49
  363.3 2.0 convolution_subtract_fusion.11
  365.4 11.9 %cholesky.546 = f32[128,128]{1,0:T(8,128)S(1)} custom-call(f32[128,128]{1,0:T(8,128)S(1)} %cholesky.609), custom_call_target="Cholesky" | custom-call | tf_op jit(solution)/shard_map/jit(cholesky)/cholesky | solution.py:49
  378.7 9.8 %custom-call.68 = f32[1,128,128]{1,2,0:T(8,128)S(1)} custom-call(f32[1,128,128]{2,1,0:T(8,128)S(1)} %get-tuple-element.62), custom_call_target="InvertDiagBlocksLowerTriangular" | custom-call | tf_op jit(solution)/shard_map/jit(cholesky)/cholesky | solution.py:49
  391.1 11.7 %cholesky.564 = f32[128,128]{1,0:T(8,128)S(1)} custom-call(f32[128,128]{1,0:T(8,128)S(1)} %convolution_subtract_fusion.12), custom_call_target="Cholesky" | custom-call | tf_op jit(solution)/shard_map/jit(cholesky)/cholesky | solution.py:49
  409.7 6.7 fusion.3
  416.4 23.3 %while.1 = (s32[]{:T(128)}, f32[1024,1024]{1,0:T(8,128)}, s32[8,2]{0,1:T(2,128)S(1)}, f32[8,128,128]{2,1,0:T(8,128)S(1)}, s32[]{:T(128)}) while((s32[]{:T(128)}, f32[1024,1024]{1,0:T(8,128)}, s32[8,2]{0,1:T(2,128)S(1)}, f32[8,128,128]{2,1,0:T(8,128)S(1)}, s32[]{:T(128)}) %tuple.72), condition=%wide.while_cond, body=%wide.while_body.sunk | while | flops 2 | bytes 131189 | solution.py:53
  417.0 2.3 bitcast_dynamic-update-slice_fusion.4
  420.0 2.3 bitcast_dynamic-update-slice_fusion.4
  422.9 2.3 bitcast_dynamic-update-slice_fusion.4
  425.8 2.3 bitcast_dynamic-update-slice_fusion.4
  428.7 2.3 bitcast_dynamic-update-slice_fusion.4
  431.6 2.3 bitcast_dynamic-update-slice_fusion.4
  434.5 2.3 bitcast_dynamic-update-slice_fusion.4
  437.5 2.2 bitcast_dynamic-update-slice_fusion.4
  439.7 79.0 %custom-call.69 = f32[8,128,128]{1,2,0:T(8,128)S(1)} custom-call(f32[8,128,128]{2,1,0:T(8,128)S(1)} %get-tuple-element.9), custom_call_target="InvertDiagBlocksLowerTriangular" | custom-call | tf_op jit(solution)/shard_map/triangular_solve | solution.py:53
  518.7 2.1 constant_dynamic-update-slice_fusion.17
  520.8 2.5 convolution_subtract_fusion.3
  524.2 3.7 convolution_subtract_fusion.5
  528.9 4.9 convolution_subtract_fusion.2
  534.9 6.2 fusion.12
  542.0 7.3 %convolution_subtract_fusion.1 = f32[1408,128]{1,0:T(8,128)S(1)} fusion(f32[1408,640]{0,1:T(8,128)S(1)} %get-tuple-element.42, f32[1408,1024]{1,0:T(8,128)} %bitcast_dynamic-update-slice_fusion.2, f32[1024,1024]{1,0:T(8,128)} %get-tuple-element.146), kind=kOutput, calls=%fused_computation.23 | convolution fusion | flops 1384300544 | bytes 5373952 | tf_op jit(solution)/shard_map/triangular_solve | solution.py:53
  550.2 8.6 %convolution_subtract_fusion = f32[1408,128]{1,0:T(8,128)S(1)} fusion(f32[1408,768]{0,1:T(8,128)S(1)} %get-tuple-element.38, f32[1408,1024]{1,0:T(8,128)} %bitcast_dynamic-update-slice_fusion.2, f32[1024,1024]{1,0:T(8,128)} %get-tuple-element.146), kind=kOutput, calls=%fused_computation.22 | convolution fusion | flops 1661124608 | bytes 6160384 | tf_op jit(solution)/shard_map/triangular_solve | solution.py:53
  559.7 10.1 %convolution_subtract_fusion.4 = f32[1408,128]{1,0:T(8,128)S(1)} fusion(f32[1408,896]{0,1:T(8,128)S(1)} %get-tuple-element.34, f32[1408,1024]{1,0:T(8,128)} %bitcast_dynamic-update-slice_fusion.2, f32[1024,1024]{1,0:T(8,128)} %get-tuple-element.146), kind=kOutput, calls=%fused_computation.26 | convolution fusion | flops 1937948672 | bytes 6946816 | tf_op jit(solution)/shard_map/triangular_solve | solution.py:53
  570.7 2.1 slice.281
  573.1 5.1 copy.62
  582.2 9.0 %fusion.23 = f32[7,128,4,128]{3,1,2,0:T(8,128)S(1)} fusion(f32[1,8,1,128,4,1,128]{6,3,4,1,5,2,0:T(8,128)} %copy-done.2, f32[7,128,1024,1]{2,1,3,0:T(8,128)} %bitcast.180, f32[4,128,1024,1]{2,1,0,3:T(8,128)} %bitcast.183, f32[7,128,128]{2,1,0:T(8,128)S(1)} %constant_dynamic-slice_fusion.2, pred[4]{0:T(512)(128)(4,1)S(1)} %get-tuple-element.92), kind=kOutput, calls=%fused_computation.42 | convolution fusion | flops 5638062080 | bytes 9895940 | tf_op jit(solution)/shard_map/atk,bsk->atbs/dot_general | solution.py:60
  591.2 2.4 copy.65
  593.6 3.7 concatenate.33
  597.4 3.8 convolution_bitcast_fusion
  601.2 6.3 copy.66
  607.5 10.2 %all-to-all-start = ((f32[16,1,65536]{2,1,0:T(1,128)}), f32[16,1,65536]{2,1,0:T(1,128)}, u32[]{:S(2)}, u32[]{:S(2)}) async-start(f32[16,1,65536]{2,1,0:T(1,128)} %copy.66), calls=%async_computation | async-start | bytes 8388608 | tf_op jit(solution)/shard_map/all_to_all | solution.py:118
  618.7 3.5 copy.69
  622.2 88.3 %all-to-all-done = f32[16,1,65536]{2,1,0:T(1,128)} async-done(((f32[16,1,65536]{2,1,0:T(1,128)}), f32[16,1,65536]{2,1,0:T(1,128)}, u32[]{:S(2)}, u32[]{:S(2)}) %all-to-all-start) | async-done | bytes 4194336 | tf_op jit(solution)/shard_map/all_to_all | solution.py:118
  710.5 7.8 %convolution_bitcast_fusion.1 = f32[4,2,65536]{2,0,1:T(4,128)} fusion(f32[16,1,65536]{2,1,0:T(1,128)} %all-to-all-done, s32[2,8]{1,0:T(2,128)S(1)} %eq.135), kind=kOutput, calls=%fused_computation.3 | convolution fusion | flops 50331712 | bytes 6291520 | tf_op jit(solution)/shard_map/slrk,lrkx->slx/dot_general | solution.py:129
  718.3 3.0 reshape.514
  721.3 2.8 fusion.27
  (111 shorter events, 50.9 us)
Async XLA Ops:
  7.2 4.2 slice-start.1
  7.2 83.8 %all-gather.8.cloned.1.call-start = ((), (), s32[]{:S(2)}) async-start(), calls=%async_computation.3 | async-start | bytes 8912896 | tf_op jit(solution)/shard_map/all_gather | solution.py:46
  9.1 1.3 copy-start.2
  11.3 118.9 %all-gather.10.cloned.1.call-start = ((), (), s32[]{:S(2)}) async-start(), calls=%async_computation.4 | async-start | bytes 2359296 | tf_op jit(solution)/shard_map/all_gather | solution.py:44
  12.1 182.5 %all-gather.6.cloned.1.call-start = ((), (), s32[]{:S(2)}) async-start(), calls=%async_computation.2 | async-start | bytes 4718592 | tf_op jit(solution)/shard_map/all_gather | solution.py:48
  91.0 2.2 slice-start
  93.2 5.4 copy-start.4
  95.6 1.9 copy-start
  99.9 507.6 %all-to-all-start.1 = ((s32[16,1,1]{2,1,0:T(1,128)}), s32[16,1,1]{2,1,0:T(1,128)S(1)}, u32[]{:S(2)}, u32[]{:S(2)}) async-start(s32[16,1,1]{2,1,0:T(1,128)} %copy.67), calls=%async_computation.1 | async-start | bytes 16384 | tf_op jit(solution)/shard_map/all_to_all | solution.py:119
  204.6 2.0 copy-start.1
  607.5 103.0 %all-to-all-start = ((f32[16,1,65536]{2,1,0:T(1,128)}), f32[16,1,65536]{2,1,0:T(1,128)}, u32[]{:S(2)}, u32[]{:S(2)}) async-start(f32[16,1,65536]{2,1,0:T(1,128)} %copy.66), calls=%async_computation | async-start | bytes 8388608 | tf_op jit(solution)/shard_map/all_to_all | solution.py:118
  622.2 99.2 %copy-start.3 = (f32[4,1,1,128,4,1,128]{6,5,4,3,2,1,0:T(1,128)S(1)}, f32[4,1,1,128,4,1,128]{6,5,4,3,2,1,0:T(1,128)}, u32[]{:S(2)}) copy-start(f32[4,1,1,128,4,1,128]{6,5,4,3,2,1,0:T(1,128)} %param.5) | copy-start | bytes 3145732
Sparse Core Ops, SparseCore 0:
  11.4 79.5 all-gather.7
  92.8 37.3 all-gather.9
  132.5 62.1 all-gather.5
where the time goes:
time: 737 us; the launch traced here: 731 us
  other arithmetic  266 us (36%)
  waiting for transfers between devices  245 us (33%)
  matrix products  98.3 us (13%)
  local copies, waits for them, and re-layouts  84.2 us (11%)
  between operations  19.4 us (3%)
  starting transfers between devices  18 us (2%)
    another operation x30, other arithmetic, per_device(): lower_factor = jnp.linalg.cholesky(diagonal_block)  172 us
    all_to_all x1, waiting for transfers between devices, per_device(): lax.all_to_all(send_buffer, ('leaf', 'row'), split_axis=0, concat_axis=0,...  88.3 us
    another operation x3, other arithmetic, per_device(): lax.linalg.triangular_solve(lower_factor, stacked, left_side=False, lower...  85.7 us
    all_gather x1, waiting for transfers between devices, per_device(): first_cols = lax.all_gather(working[:, :, 0, :], 'col', axis=0, tiled=False)  78.9 us
    all_gather x1, waiting for transfers between devices, per_device(): diagonal_block = lax.all_gather(row_panel[0], 'row', axis=0, tiled=True)  55.7 us
    another operation x15, matrix products, per_device(): lax.linalg.triangular_solve(lower_factor, stacked, left_side=False, lower...  51.9 us
    another operation x24, local copies, waits for them, and re-layouts  23.1 us
    another operation x14, matrix products, per_device(): lower_factor = jnp.linalg.cholesky(diagonal_block)  23.1 us
  transfers between devices with their start and end apart: 5, of which 4 were waited for; matrix products, arithmetic and copies ran while one was open for 58% of the time, Pallas kernels for 0%

commit v1 on v0

--- a/solution.py
+++ b/solution.py
@@ -45,7 +45,9 @@
     column_panel = top_rows.transpose(2, 3, 0, 1).reshape(col_slots, TILE, NPIV)
     first_cols = lax.all_gather(working[:, :, 0, :], "col", axis=0, tiled=False)
     row_panel = first_cols[:pivot_tiles].transpose(1, 2, 0, 3).reshape(row_slots, TILE, NPIV)
-    diagonal_block = lax.all_gather(row_panel[0], "row", axis=0, tiled=True)
+    diagonal_block = jnp.concatenate(
+        lax.all_to_all(jnp.stack([row_panel[0]] * lax.axis_size("row")), "row", 0, 0), axis=0
+    )
     lower_factor = jnp.linalg.cholesky(diagonal_block)
     stacked = jnp.concatenate(
         [row_panel[1:].reshape(-1, NPIV), column_panel.reshape(-1, NPIV)], axis=0

time: 737 us -> 771 us (1.046)
  waiting for transfers between devices: 245 us -> 271 us
    all_gather x1, waiting for transfers between devices: 22.4 us -> 85.5 us  [per_device(): top_rows = lax.all_gather(working[0], 'row', axis=0, tiled=False)]
    all_gather x1 -> x0, waiting for transfers between devices: 55.7 us -> none  [per_device(): diagonal_block = lax.all_gather(row_panel[0], 'row', axis=0, tiled=True)]
    all_to_all x0 -> x1, waiting for transfers between devices: none -> 17.6 us  [per_device(): lax.all_to_all(jnp.stack([row_panel[0]] * lax.axis_size('row')), 'row', 0...]
    reshape x0 -> x2, local copies, waits for them, and re-layouts: none -> 10.2 us  [per_device(): jnp.concatenate(lax.all_to_all(jnp.stack([row_panel[0]] * lax.axis_size('...]
    another operation x24 -> x25, local copies, waits for them, and re-layouts: 23.1 us -> 25.5 us
  transfers between devices with their start and end apart: 5 -> 5, of which waited for: 4 -> 4; matrix products, arithmetic and copies ran while one was open for 58% -> 56% of each run, Pallas kernels for 0% -> 0%
where the time goes in v1:
time: 771 us; the launch traced here: 765 us
  waiting for transfers between devices  271 us (35%)
  other arithmetic  265 us (34%)
  matrix products  98.5 us (13%)
  local copies, waits for them, and re-layouts  90.6 us (12%)
  between operations  21.1 us (3%)
  starting transfers between devices  18.3 us (2%)
    another operation x30, other arithmetic, per_device(): lower_factor = jnp.linalg.cholesky(diagonal_block)  172 us
    all_to_all x1, waiting for transfers between devices, per_device(): lax.all_to_all(send_buffer, ('leaf', 'row'), split_axis=0, concat_axis=0,...  88.1 us
    another operation x3, other arithmetic, per_device(): lax.linalg.triangular_solve(lower_factor, stacked, left_side=False, lower...  85.7 us
    all_gather x1, waiting for transfers between devices, per_device(): top_rows = lax.all_gather(working[0], 'row', axis=0, tiled=False)  85.5 us
    all_gather x1, waiting for transfers between devices, per_device(): first_cols = lax.all_gather(working[:, :, 0, :], 'col', axis=0, tiled=False)  79.7 us
    another operation x15, matrix products, per_device(): lax.linalg.triangular_solve(lower_factor, stacked, left_side=False, lower...  51.9 us
    another operation x14, matrix products, per_device(): lower_factor = jnp.linalg.cholesky(diagonal_block)  23.2 us
    another operation x24, local copies, waits for them, and re-layouts  23.1 us
  transfers between devices with their start and end apart: 5, of which 4 were waited for; matrix products, arithmetic and copies ran while one was open for 56% of the time, Pallas kernels for 0%

profile of v1, /device:TPU:1, one launch (start us, length us, event | category | flops | bytes accessed | tf_op | source)
XLA Modules:
  0.0 764.6 jit_solution(17324432708847414662)
XLA Ops:
  12.1 79.7 %all-gather.5.cloned.1.call-done = f32[128,128,1,128]{3,1,2,0:T(8,128)} async-done(((f32[8,128,1,128]{3,1,2,0:T(8,128)}), f32[128,128,1,128]{3,1,2,0:T(8,128)}) %all-gather.5.cloned.1.call-update) | async-done | bytes 8388624 | tf_op jit(solution)/shard_map/all_gather | solution.py:46
  91.8 2.5 slice.281
  96.4 2.3 stack.3
  98.8 6.9 all-to-all-start
  107.9 85.5 %all-gather.7.cloned.1.call-done = f32[8,1,1,128,4,1,128]{6,3,5,4,2,1,0:T(8,128)} async-done(((f32[1,1,1,128,4,1,128]{6,3,5,4,2,1,0:T(8,128)}), f32[8,1,1,128,4,1,128]{6,3,5,4,2,1,0:T(8,128)}) %all-gather.7.cloned.1.call-update) | async-done | bytes 2097168 | tf_op jit(solution)/shard_map/all_gather | solution.py:44
  195.4 2.5 slice.283
  200.0 2.7 bitcast_dynamic-update-slice_fusion.1
  204.4 17.6 %all-to-all-done = f32[8,128,1024]{1,2,0:T(8,128)} async-done(((f32[8,128,1024]{1,2,0:T(8,128)}), f32[8,128,1024]{1,2,0:T(8,128)}, u32[]{:S(2)}, u32[]{:S(2)}) %all-to-all-start) | async-done | bytes 4194336 | tf_op jit(solution)/shard_map/all_to_all | solution.py:49
  222.0 3.8 all-to-all-start.2
  225.9 4.7 copy_bitcast_fusion
  230.6 5.5 copy.74
  236.1 4.1 fusion.2
  242.2 11.7 %cholesky.223 = f32[128,128]{1,0:T(8,128)S(1)} custom-call(f32[128,128]{1,0:T(8,128)S(1)} %cholesky.580), custom_call_target="Cholesky" | custom-call | tf_op jit(solution)/shard_map/jit(cholesky)/cholesky | solution.py:51
  254.0 9.8 %custom-call.62 = f32[1,128,128]{1,2,0:T(8,128)S(1)} custom-call(f32[1,128,128]{2,1,0:T(8,128)S(1)} %get-tuple-element.82), custom_call_target="InvertDiagBlocksLowerTriangular" | custom-call | tf_op jit(solution)/shard_map/jit(cholesky)/cholesky | solution.py:51
  263.8 2.5 cholesky.255
  266.3 2.4 constant_dynamic-update-slice_fusion.30
  270.2 11.7 %cholesky.244 = f32[128,128]{1,0:T(8,128)S(1)} custom-call(f32[128,128]{1,0:T(8,128)S(1)} %cholesky.584), custom_call_target="Cholesky" | custom-call | tf_op jit(solution)/shard_map/jit(cholesky)/cholesky | solution.py:51
  282.6 10.0 %custom-call.63 = f32[1,128,128]{1,2,0:T(8,128)S(1)} custom-call(f32[1,128,128]{2,1,0:T(8,128)S(1)} %get-tuple-element.79), custom_call_target="InvertDiagBlocksLowerTriangular" | custom-call | tf_op jit(solution)/shard_map/jit(cholesky)/cholesky | solution.py:51
  293.8 2.1 convolution_subtract_fusion.7
  295.9 11.7 %cholesky.468 = f32[128,128]{1,0:T(8,128)S(1)} custom-call(f32[128,128]{1,0:T(8,128)S(1)} %cholesky.589), custom_call_target="Cholesky" | custom-call | tf_op jit(solution)/shard_map/jit(cholesky)/cholesky | solution.py:51
  308.9 9.8 %custom-call.64 = f32[1,128,128]{1,2,0:T(8,128)S(1)} custom-call(f32[1,128,128]{2,1,0:T(8,128)S(1)} %get-tuple-element.76), custom_call_target="InvertDiagBlocksLowerTriangular" | custom-call | tf_op jit(solution)/shard_map/jit(cholesky)/cholesky | solution.py:51
  319.9 2.3 convolution_subtract_fusion.8
  322.2 12.1 %cholesky.487 = f32[128,128]{1,0:T(8,128)S(1)} custom-call(f32[128,128]{1,0:T(8,128)S(1)} %cholesky.594), custom_call_target="Cholesky" | custom-call | tf_op jit(solution)/shard_map/jit(cholesky)/cholesky | solution.py:51
  335.6 9.8 %custom-call.65 = f32[1,128,128]{1,2,0:T(8,128)S(1)} custom-call(f32[1,128,128]{2,1,0:T(8,128)S(1)} %get-tuple-element.73), custom_call_target="InvertDiagBlocksLowerTriangular" | custom-call | tf_op jit(solution)/shard_map/jit(cholesky)/cholesky | solution.py:51
  346.5 2.3 convolution_subtract_fusion.9
  348.9 11.7 %cholesky.506 = f32[128,128]{1,0:T(8,128)S(1)} custom-call(f32[128,128]{1,0:T(8,128)S(1)} %cholesky.599), custom_call_target="Cholesky" | custom-call | tf_op jit(solution)/shard_map/jit(cholesky)/cholesky | solution.py:51
  362.0 9.8 %custom-call.66 = f32[1,128,128]{1,2,0:T(8,128)S(1)} custom-call(f32[1,128,128]{2,1,0:T(8,128)S(1)} %get-tuple-element.70), custom_call_target="InvertDiagBlocksLowerTriangular" | custom-call | tf_op jit(solution)/shard_map/jit(cholesky)/cholesky | solution.py:51
  373.0 2.3 convolution_subtract_fusion.10
  375.3 11.7 %cholesky.526 = f32[128,128]{1,0:T(8,128)S(1)} custom-call(f32[128,128]{1,0:T(8,128)S(1)} %cholesky.604), custom_call_target="Cholesky" | custom-call | tf_op jit(solution)/shard_map/jit(cholesky)/cholesky | solution.py:51
  388.2 9.8 %custom-call.67 = f32[1,128,128]{1,2,0:T(8,128)S(1)} custom-call(f32[1,128,128]{2,1,0:T(8,128)S(1)} %get-tuple-element.67), custom_call_target="InvertDiagBlocksLowerTriangular" | custom-call | tf_op jit(solution)/shard_map/jit(cholesky)/cholesky | solution.py:51
  401.0 11.7 %cholesky.546 = f32[128,128]{1,0:T(8,128)S(1)} custom-call(f32[128,128]{1,0:T(8,128)S(1)} %cholesky.609), custom_call_target="Cholesky" | custom-call | tf_op jit(solution)/shard_map/jit(cholesky)/cholesky | solution.py:51
  414.1 9.9 %custom-call.68 = f32[1,128,128]{1,2,0:T(8,128)S(1)} custom-call(f32[1,128,128]{2,1,0:T(8,128)S(1)} %get-tuple-element.64), custom_call_target="InvertDiagBlocksLowerTriangular" | custom-call | tf_op jit(solution)/shard_map/jit(cholesky)/cholesky | solution.py:51
  426.7 11.7 %cholesky.564 = f32[128,128]{1,0:T(8,128)S(1)} custom-call(f32[128,128]{1,0:T(8,128)S(1)} %convolution_subtract_fusion.12), custom_call_target="Cholesky" | custom-call | tf_op jit(solution)/shard_map/jit(cholesky)/cholesky | solution.py:51
  445.3 6.7 fusion.3
  452.0 23.3 %while.1 = (s32[]{:T(128)}, f32[1024,1024]{1,0:T(8,128)}, s32[8,2]{0,1:T(2,128)S(1)}, f32[8,128,128]{2,1,0:T(8,128)S(1)}, s32[]{:T(128)}) while((s32[]{:T(128)}, f32[1024,1024]{1,0:T(8,128)}, s32[8,2]{0,1:T(2,128)S(1)}, f32[8,128,128]{2,1,0:T(8,128)S(1)}, s32[]{:T(128)}) %tuple.73), condition=%wide.while_cond, body=%wide.while_body.sunk | while | flops 2 | bytes 131189 | solution.py:55
  452.6 2.3 bitcast_dynamic-update-slice_fusion.4
  455.5 2.3 bitcast_dynamic-update-slice_fusion.4
  458.5 2.3 bitcast_dynamic-update-slice_fusion.4
  461.4 2.3 bitcast_dynamic-update-slice_fusion.4
  464.3 2.3 bitcast_dynamic-update-slice_fusion.4
  467.2 2.3 bitcast_dynamic-update-slice_fusion.4
  470.1 2.3 bitcast_dynamic-update-slice_fusion.4
  473.1 2.2 bitcast_dynamic-update-slice_fusion.4
  475.3 79.0 %custom-call.69 = f32[8,128,128]{1,2,0:T(8,128)S(1)} custom-call(f32[8,128,128]{2,1,0:T(8,128)S(1)} %get-tuple-element.9), custom_call_target="InvertDiagBlocksLowerTriangular" | custom-call | tf_op jit(solution)/shard_map/triangular_solve | solution.py:55
  556.4 2.5 convolution_subtract_fusion.3
  559.8 3.7 convolution_subtract_fusion.5
  564.5 4.9 convolution_subtract_fusion.2
  570.5 6.2 fusion.12
  577.6 7.3 convolution_subtract_fusion.1
  585.8 8.6 %convolution_subtract_fusion = f32[1408,128]{1,0:T(8,128)S(1)} fusion(f32[1408,768]{0,1:T(8,128)S(1)} %get-tuple-element.40, f32[1408,1024]{1,0:T(8,128)} %bitcast_dynamic-update-slice_fusion.2, f32[1024,1024]{1,0:T(8,128)} %get-tuple-element.147), kind=kOutput, calls=%fused_computation.22 | convolution fusion | flops 1661124608 | bytes 6160384 | tf_op jit(solution)/shard_map/triangular_solve | solution.py:55
  595.3 10.1 %convolution_subtract_fusion.4 = f32[1408,128]{1,0:T(8,128)S(1)} fusion(f32[1408,896]{0,1:T(8,128)S(1)} %get-tuple-element.36, f32[1408,1024]{1,0:T(8,128)} %bitcast_dynamic-update-slice_fusion.2, f32[1024,1024]{1,0:T(8,128)} %get-tuple-element.147), kind=kOutput, calls=%fused_computation.26 | convolution fusion | flops 1937948672 | bytes 6946816 | tf_op jit(solution)/shard_map/triangular_solve | solution.py:55
  606.3 2.1 slice.284
  608.7 5.1 copy.78
  617.8 9.0 %fusion.23 = f32[7,128,4,128]{3,1,2,0:T(8,128)S(1)} fusion(f32[1,8,1,128,4,1,128]{6,3,4,1,5,2,0:T(8,128)} %copy-done.2, f32[7,128,1024,1]{2,1,3,0:T(8,128)} %bitcast.188, f32[4,128,1024,1]{2,1,0,3:T(8,128)} %bitcast.191, f32[7,128,128]{2,1,0:T(8,128)S(1)} %constant_dynamic-slice_fusion.2, pred[4]{0:T(512)(128)(4,1)S(1)} %get-tuple-element.94), kind=kOutput, calls=%fused_computation.42 | convolution fusion | flops 5638062080 | bytes 9895940 | tf_op jit(solution)/shard_map/atk,bsk->atbs/dot_general | solution.py:62
  626.8 2.4 copy.81
  629.2 3.7 concatenate.33
  633.0 3.8 convolution_bitcast_fusion
  636.8 6.3 copy.82
  643.1 7.6 all-to-all-start.1
  651.7 3.5 copy.85
  655.2 88.1 %all-to-all-done.1 = f32[16,1,65536]{2,1,0:T(1,128)} async-done(((f32[16,1,65536]{2,1,0:T(1,128)}), f32[16,1,65536]{2,1,0:T(1,128)}, u32[]{:S(2)}, u32[]{:S(2)}) %all-to-all-start.1) | async-done | bytes 4194336 | tf_op jit(solution)/shard_map/all_to_all | solution.py:120
  743.3 7.8 %convolution_bitcast_fusion.1 = f32[4,2,65536]{2,0,1:T(4,128)} fusion(f32[16,1,65536]{2,1,0:T(1,128)} %all-to-all-done.1, s32[2,8]{1,0:T(2,128)S(1)} %eq.135), kind=kOutput, calls=%fused_computation.3 | convolution fusion | flops 50331712 | bytes 6291520 | tf_op jit(solution)/shard_map/slrk,lrkx->slx/dot_general | solution.py:131
  751.1 3.0 reshape.519
  754.1 2.8 fusion.27
  (111 shorter events, 56.3 us)
Async XLA Ops:
  8.0 83.8 %all-gather.5.cloned.1.call-start = ((), (), s32[]{:S(2)}) async-start(), calls=%async_computation.3 | async-start | bytes 8912896 | tf_op jit(solution)/shard_map/all_gather | solution.py:46
  9.9 1.3 copy-start.2
  94.3 1.9 copy-start
  98.8 6.9 slice-start
  98.8 7.7 %copy-start.4 = (s32[2,56]{1,0:T(2,128)S(1)}, s32[2,56]{1,0:T(2,128)}, u32[]{:S(2)}) copy-start(s32[2,56]{1,0:T(2,128)} %param.6) | copy-start | bytes 1348
  98.8 123.3 %all-to-all-start = ((f32[8,128,1024]{1,2,0:T(8,128)}), f32[8,128,1024]{1,2,0:T(8,128)}, u32[]{:S(2)}, u32[]{:S(2)}) async-start(f32[8,128,1024]{1,2,0:T(8,128)} %stack.3), calls=%async_computation | async-start | bytes 8388608 | tf_op jit(solution)/shard_map/all_to_all | solution.py:49
  105.7 87.7 %all-gather.7.cloned.1.call-start = ((), (), s32[]{:S(2)}) async-start(), calls=%async_computation.4 | async-start | bytes 2359296 | tf_op jit(solution)/shard_map/all_gather | solution.py:44
  222.0 421.0 %all-to-all-start.2 = ((s32[16,1,1]{2,1,0:T(1,128)}), s32[16,1,1]{2,1,0:T(1,128)S(1)}, u32[]{:S(2)}, u32[]{:S(2)}) async-start(s32[16,1,1]{2,1,0:T(1,128)} %copy.83), calls=%async_computation.2 | async-start | bytes 16384 | tf_op jit(solution)/shard_map/all_to_all | solution.py:121
  240.2 2.0 copy-start.1
  643.1 100.2 %all-to-all-start.1 = ((f32[16,1,65536]{2,1,0:T(1,128)}), f32[16,1,65536]{2,1,0:T(1,128)}, u32[]{:S(2)}, u32[]{:S(2)}) async-start(f32[16,1,65536]{2,1,0:T(1,128)} %copy.82), calls=%async_computation.1 | async-start | bytes 8388608 | tf_op jit(solution)/shard_map/all_to_all | solution.py:120
  655.2 98.9 %copy-start.3 = (f32[4,1,1,128,4,1,128]{6,5,4,3,2,1,0:T(1,128)S(1)}, f32[4,1,1,128,4,1,128]{6,5,4,3,2,1,0:T(1,128)}, u32[]{:S(2)}) copy-start(f32[4,1,1,128,4,1,128]{6,5,4,3,2,1,0:T(1,128)} %param.5) | copy-start | bytes 3145732
Sparse Core Ops, SparseCore 0:
  12.2 79.5 all-gather.4
Sparse Core Ops, SparseCore 1:
  108.5 84.8 all-gather.6
